TPU v7x, 256 devices: a whole 4x4x8 slice. The times are simulated.
256 devices in a mesh: rep: 32 (over x, y, core), tp: 8 (over z).
Axes of the slice: x: 4, y: 4, z: 8, core: 2. Of those that a mesh axis runs over, the one named last changes fastest.
Arguments:
- prompt_rows: bfloat16 [20480, 2048], P(('rep', 'tp')), may hold values from -6 to 6
- prompt_pieces: int32 [32, 640], P('rep'), may hold values from 0 to 9, never falling along the last dimension, each value on 1 to 320 neighbouring positions
- decode_rows: bfloat16 [1280, 2048], P('rep'), may hold values from -6 to 6
- request_ages: int32 [1280], P('rep'), may hold values from 2 to 127
- migrate_to: int32 [512, 1], P('rep'), may hold values from 0 to 31, as said below
- past_cache: bfloat16 [1280, 2, 128, 2048], P('rep', None, None, 'tp'), may hold values from -8 to 8
- norm_gain: float32 [2048], replicated, may hold values from 0.5 to 1.5
- norm_bias: float32 [2048], replicated, may hold values from -2 to 2
- qkv_weight: bfloat16 [3, 2048, 2048], P(None, None, 'tp'), may hold values from -0.125 to 0.125
- qkv_bias: float32 [3, 2048], P(None, 'tp'), may hold values from -4 to 4
- out_weight: bfloat16 [2048, 2048], P('tp'), may hold values from -0.125 to 0.125
- out_bias: float32 [2048], replicated, may hold values from -3 to 3
Outputs:
- prompt_out: bfloat16 [20480, 2048], P(('rep', 'tp'))
- prompt_cache: bfloat16 [2, 20480, 2048], P(None, 'rep', 'tp')
- kept_out: bfloat16 [768, 2048], P('rep')
- kept_cache: bfloat16 [768, 2, 128, 2048], P('rep', None, None, 'tp')
- moved_out: bfloat16 [1024, 2048], P('rep')
- moved_cache: bfloat16 [1024, 2, 128, 2048], P('rep', None, None, 'tp')
Inputs may be any that keep to these rules, and one draw needn't show every extreme that they name: `migrate_to`: the 16 requests that leave one replica name 16 different target replicas, and one target replica is named by every replica. `prompt_pieces`: piece numbers never fall along a replica's prompt tokens; a piece has at most 320 tokens, and some piece exactly that many.
All inputs are finite; a program needn't handle non-finite values.
Results may differ from a plain program's by a relative error of at most 0.014.
Values may be sent and summed in bfloat16 or wider, within the bound.
No kernel may reach another device: no remote copies, remote signals or barrier semaphores. Data moves between devices by JAX's collectives and lax.ppermute only.
A program may use at most 128 MiB of HBM per device.

v0:
```python
import jax
import jax.numpy as jnp
from jax import lax
from jax.sharding import PartitionSpec as P

HEAD_DIM = 128
CAP = 1
EPSILON = 1e-05


def layer_norm(values, norm_gain, norm_bias):
    wide = values.astype(jnp.float32)
    center = jnp.mean(wide, axis=-1, keepdims=True)
    spread = jnp.mean(jnp.square(wide - center), axis=-1, keepdims=True)
    scaled = (wide - center) * lax.rsqrt(spread + EPSILON)
    return (scaled * norm_gain + norm_bias).astype(jnp.bfloat16)


def decode_partial(
    rows, cache, live, position, norm_gain, norm_bias, qkv_weight, qkv_bias, out_weight
):
    count = rows.shape[0]
    width = qkv_weight.shape[2]
    heads_here = width // HEAD_DIM
    length = cache.shape[2]
    normed = layer_norm(rows, norm_gain, norm_bias)
    projected = jnp.einsum("rd,cde->cre", normed, qkv_weight, preferred_element_type=jnp.float32)
    queries = (projected[0] + qkv_bias[0]).astype(jnp.bfloat16).reshape(count, heads_here, HEAD_DIM)
    key_new = (projected[1] + qkv_bias[1]).astype(jnp.bfloat16)
    value_new = (projected[2] + qkv_bias[2]).astype(jnp.bfloat16)
    old_keys = cache[:, 0].reshape(count, length, heads_here, HEAD_DIM)
    old_values = cache[:, 1].reshape(count, length, heads_here, HEAD_DIM)
    scale = HEAD_DIM ** (-0.5)
    scores = (
        jnp.einsum("rhe,rlhe->rhl", queries, old_keys, preferred_element_type=jnp.float32) * scale
    )
    own = (
        jnp.sum(
            queries.astype(jnp.float32)
            * key_new.astype(jnp.float32).reshape(count, heads_here, HEAD_DIM),
            axis=-1,
        )
        * scale
    )
    scores = jnp.where(live[:, None, :], scores, -1e30)
    highest = jnp.maximum(jnp.max(scores, axis=-1), own)
    weights = jnp.exp(scores - highest[..., None])
    own_weight = jnp.exp(own - highest)
    total = jnp.sum(weights, axis=-1) + own_weight
    probs = (weights / total[..., None]).astype(jnp.bfloat16)
    own_prob = (own_weight / total).astype(jnp.bfloat16)
    context = jnp.einsum("rhl,rlhe->rhe", probs, old_values, preferred_element_type=jnp.float32)
    context = context + own_prob.astype(jnp.float32)[..., None] * value_new.astype(
        jnp.float32
    ).reshape(count, heads_here, HEAD_DIM)
    context = context.reshape(count, width).astype(jnp.bfloat16)
    partial_value = jnp.dot(context, out_weight, preferred_element_type=jnp.float32)
    written = (jnp.arange(length)[None, :] == position[:, None])[:, :, None]
    new_keys = jnp.where(written, key_new[:, None, :], cache[:, 0])
    new_values = jnp.where(written, value_new[:, None, :], cache[:, 1])
    return (partial_value, jnp.stack([new_keys, new_values], axis=1))


def on_device(
    prompt_rows,
    prompt_pieces,
    decode_rows,
    request_ages,
    migrate_to,
    past_cache,
    norm_gain,
    norm_bias,
    qkv_weight,
    qkv_bias,
    out_weight,
    out_bias,
):
    rep_count = lax.axis_size("rep")
    width = qkv_weight.shape[2]
    heads_here = width // HEAD_DIM
    length = past_cache.shape[2]
    leaving = migrate_to.shape[0]
    staying = decode_rows.shape[0] - leaving
    slot_count = rep_count * CAP
    normed = layer_norm(lax.all_gather(prompt_rows, "tp", axis=0, tiled=True), norm_gain, norm_bias)
    projected = jnp.einsum("rd,cde->cre", normed, qkv_weight, preferred_element_type=jnp.float32)
    total_rows = projected.shape[1]
    queries = (projected[0] + qkv_bias[0]).astype(jnp.bfloat16)
    key_rows = (projected[1] + qkv_bias[1]).astype(jnp.bfloat16)
    value_rows = (projected[2] + qkv_bias[2]).astype(jnp.bfloat16)
    head_q = queries.reshape(total_rows, heads_here, HEAD_DIM)
    head_k = key_rows.reshape(total_rows, heads_here, HEAD_DIM)
    head_v = value_rows.reshape(total_rows, heads_here, HEAD_DIM)
    scores = jnp.einsum(
        "qhe,khe->hqk", head_q, head_k, preferred_element_type=jnp.float32
    ) * HEAD_DIM ** (-0.5)
    pieces = prompt_pieces[0]
    position = jnp.arange(total_rows)
    allowed = (pieces[:, None] == pieces[None, :]) & (position[None, :] <= position[:, None])
    scores = jnp.where(allowed[None], scores, -1e30)
    highest = jnp.max(scores, axis=-1, keepdims=True)
    weights = jnp.exp(scores - highest)
    probs = (weights / jnp.sum(weights, axis=-1, keepdims=True)).astype(jnp.bfloat16)
    context = jnp.einsum("hqk,khe->qhe", probs, head_v, preferred_element_type=jnp.float32)
    context = context.reshape(total_rows, width).astype(jnp.bfloat16)
    attended = lax.psum_scatter(
        jnp.dot(context, out_weight, preferred_element_type=jnp.float32).astype(jnp.bfloat16),
        "tp",
        scatter_dimension=0,
        tiled=True,
    ).astype(jnp.float32)
    prompt_out = (prompt_rows.astype(jnp.float32) + attended + out_bias).astype(jnp.bfloat16)
    prompt_cache = jnp.stack([key_rows, value_rows])
    targets = migrate_to[:, 0]
    onehot = (targets[:, None] == jnp.arange(rep_count)[None, :]).astype(jnp.float32)
    lower = (jnp.arange(leaving)[:, None] > jnp.arange(leaving)[None, :]).astype(jnp.float32)
    earlier = jnp.dot(lower, onehot)
    rank = jnp.sum(earlier * onehot, axis=1).astype(jnp.int32)
    slot = targets * CAP + rank
    placing = (jnp.arange(slot_count)[:, None] == slot[None, :]).astype(jnp.bfloat16)
    cells = jnp.arange(length)
    live = cells[None, :] < request_ages[:, None]
    partial_value, updated = decode_partial(
        decode_rows,
        past_cache,
        live,
        request_ages,
        norm_gain,
        norm_bias,
        qkv_weight,
        qkv_bias,
        out_weight,
    )
    summed = lax.psum(partial_value.astype(jnp.bfloat16), "tp").astype(jnp.float32)
    decode_out = (decode_rows.astype(jnp.float32) + summed + out_bias).astype(jnp.bfloat16)
    kept_out = decode_out[:staying]
    kept_cache = updated[:staying]
    send_cache = jnp.einsum(
        "so,oklh->sklh", placing, updated[staying:], preferred_element_type=jnp.float32
    ).astype(jnp.bfloat16)
    send_rows = jnp.dot(placing, decode_out[staying:], preferred_element_type=jnp.float32).astype(
        jnp.bfloat16
    )
    moved_cache, moved_out = (
        lax.all_to_all(send_cache, "rep", split_axis=0, concat_axis=0, tiled=True),
        lax.all_to_all(send_rows, "rep", split_axis=0, concat_axis=0, tiled=True),
    )
    return (prompt_out, prompt_cache, kept_out, kept_cache, moved_out, moved_cache)


def solution(mesh):
    placed = (
        P(("rep", "tp"), None),
        P("rep", None),
        P("rep", None),
        P("rep"),
        P("rep", None),
        P("rep", None, None, "tp"),
        P(),
        P(),
        P(None, None, "tp"),
        P(None, "tp"),
        P("tp", None),
        P(),
    )
    return jax.shard_map(
        on_device,
        mesh=mesh,
        in_specs=placed,
        out_specs=(
            P(("rep", "tp"), None),
            P(None, "rep", "tp"),
            P("rep", None),
            P("rep", None, None, "tp"),
            P("rep", None),
            P("rep", None, None, "tp"),
        ),
        check_vma=False,
    )
```

profile of v0, /device:TPU:8, one launch (start us, length us, event | category | flops | bytes accessed | tf_op | source)
XLA Modules:
  0.0 225.0 jit_solution(8399299144730349695)
XLA Ops:
  11.1 1.6 convolution_bitcast_fusion
  13.1 5.5 %fusion.71 = (bf16[40,1,128,256]{3,2,1,0:T(8,128)(2,1)}, bf16[40,1,128,256]{3,2,1,0:T(8,128)(2,1)}) fusion(bf16[40,2,128,256]{3,2,1,0:T(8,128)(2,1)} %param.17), kind=kLoop, calls=%fused_computation.117 | loop fusion | bytes 10485760 | tf_op jit(solution)/shard_map/slice | solution.py:31
  18.6 4.4 %copy.84 = bf16[40,1,128,256]{2,3,0,1:T(8,128)(2,1)} copy(bf16[40,1,128,256]{3,2,1,0:T(8,128)(2,1)} %get-tuple-element.36) | data formatting | bytes 5242880 | tf_op jit(solution)/shard_map/reshape;squeeze | solution.py:31
  23.0 2.6 %fusion.53 = f32[40,2,1,128]{3,2,1,0:T(1,128)S(1)} fusion(bf16[40,128,2,128]{1,3,2,0:T(8,128)(2,1)} %bitcast.75, bf16[40,2,128,1]{2,1,0,3:T(2,128)(2,1)S(1)} %get-tuple-element.49), kind=kOutput, calls=%fused_computation.82 | convolution fusion | flops 2621440 | bytes 2682880 | tf_op jit(solution)/shard_map/rhe,rlhe->rhl/dot_general | solution.py:35
  26.1 4.9 %reshape.266 = bf16[40,128,2,128]{3,2,1,0:T(2,128)(2,1)} reshape(bf16[40,1,128,256]{3,2,1,0:T(8,128)(2,1)} %get-tuple-element.37) | data formatting | bytes 5242880 | tf_op jit(solution)/shard_map/reshape;squeeze | solution.py:32
  31.1 4.4 %fusion.11 = f32[40,2,1,128]{3,2,1,0:T(1,128)S(1)} fusion(bf16[40,2,128,1]{2,0,1,3:T(8,128)(2,1)S(1)} %fusion.59, bf16[40,128,2,128]{3,2,1,0:T(2,128)(2,1)} %reshape.266), kind=kOutput, calls=%fused_computation.20 | convolution fusion | flops 2621440 | bytes 2682880 | tf_op jit(solution)/shard_map/rhl,rlhe->rhe/dot_general | solution.py:52
  38.3 8.5 %broadcast_select_fusion = (bf16[40,1,128,256]{3,0,2,1:T(8,128)(2,1)}, bf16[40,1,128,256]{3,0,2,1:T(8,128)(2,1)}) fusion(pred[40,128]{0,1:T(8,128)(4,1)S(1)} %get-tuple-element.57, bf16[40,256]{1,0:T(8,128)(2,1)S(1)} %get-tuple-element.43, bf16[40,1,128,256]{3,2,1,0:T(8,128)(2,1)} %get-tuple-element.37, bf16[40,1,128,256]{3,2,1,0:T(8,128)(2,1)} %get-tuple-element.36, ...), kind=kLoop, calls=%fused_computation.26 | loop fusion | flops 2621440 | bytes 10531840 | tf_op jit(solution)/shard_map/jit(_where)/select_n | solution.py:60
  46.8 8.3 %all-gather.2.cloned.1.call-done = bf16[640,2048]{1,0:T(8,128)(2,1)} async-done(((bf16[80,2048]{1,0:T(8,128)(2,1)}), bf16[640,2048]{1,0:T(8,128)(2,1)}) %all-gather.2.cloned.1.call-update) | async-done | bytes 2621456 | tf_op jit(solution)/shard_map/all_gather | solution.py:85
  55.1 2.3 %convert_reduce_fusion = f32[640]{0:T(1024)S(1)} fusion(bf16[640,2048]{1,0:T(8,128)(2,1)} %all-gather.2.cloned.1.call-done), kind=kLoop, calls=%fused_computation.2 | loop fusion | flops 2620800 | bytes 2624000 | tf_op jit(solution)/shard_map/reduce_sum | solution.py:13
  58.4 3.1 %fusion.25 = f32[3,640,256]{1,2,0:T(8,128)S(1)} fusion(bf16[3,2048,256]{2,1,0:T(8,128)(2,1)S(1)} %copy-done, bf16[640,2048]{1,0:T(8,128)(2,1)S(1)} %copy-done.3, f32[2048]{0:T(1024)S(1)} %copy-done.12, f32[2048]{0:T(1024)S(1)} %copy-done.13, f32[640]{0:T(1024)S(1)} %add_rsqrt_fusion, f32[640]{0:T(1024)S(1)} %broadcast_multiply_fusion), kind=kOutput, calls=%fused_computation.39 | convolution fusion | flops 2021130240 | bytes 7754752 | tf_op jit(solution)/shard_map/rd,cde->cre/dot_general | solution.py:86
  63.2 2.0 fusion.74
  66.4 2.4 %convolution_convert_fusion = bf16[640,2048]{1,0:T(8,128)(2,1)} fusion(bf16[640,256]{0,1:T(8,128)(2,1)S(1)} %bitcast.78, bf16[256,2048]{1,0:T(8,128)(2,1)S(1)} %copy-done.5), kind=kOutput, calls=%fused_computation.14 | convolution fusion | flops 672399360 | bytes 3997696 | tf_op jit(solution)/shard_map/dot_general | solution.py:107
  68.9 60.0 %all-reduce.2.cloned.1.call-done = bf16[40,2048]{1,0:T(8,128)(2,1)} async-done(((bf16[40,2048]{1,0:T(8,128)(2,1)}), bf16[40,2048]{1,0:T(8,128)(2,1)}) %all-reduce.2.cloned.1.call-update) | async-done | bytes 163856 | tf_op jit(solution)/shard_map/psum | solution.py:134
  131.3 1.3 reduce.1
  132.6 1.6 reshape.267
  134.3 7.4 %all-to-all-start = ((bf16[32,2,1024]{2,1,0:T(2,128)(2,1)}), bf16[32,2,1024]{2,1,0:T(2,128)(2,1)S(1)}, u32[]{:S(2)}, u32[]{:S(2)}) async-start(bf16[32,2,1024]{2,1,0:T(2,128)(2,1)} %reshape.267), calls=%async_computation.1 | async-start | bytes 262144 | tf_op jit(solution)/shard_map/all_to_all | solution.py:146
  141.7 2.6 %convolution_convert_fusion.1 = bf16[32,2,128,256]{3,0,2,1:T(8,128)(2,1)S(1)} fusion(bf16[40,1,128,256]{3,0,2,1:T(8,128)(2,1)S(1)} %copy-done.2, bf16[40,1,128,256]{3,0,2,1:T(8,128)(2,1)} %get-tuple-element.51, s32[16]{0:T(128)S(1)} %convert_add_fusion.1), kind=kOutput, calls=%fused_computation.16 | convolution fusion | flops 73400832 | bytes 9437248 | tf_op jit(solution)/shard_map/so,oklh->sklh/dot_general | solution.py:138
  144.3 4.4 %copy.72 = bf16[32,2,128,256]{3,2,1,0:T(8,128)(2,1)} copy(bf16[32,2,128,256]{3,0,2,1:T(8,128)(2,1)S(1)} %convolution_convert_fusion.1) | data formatting | bytes 8388608 | tf_op jit(solution)/shard_map/convert_element_type | solution.py:140
  148.7 7.4 %all-to-all-start.1 = ((bf16[32,2,128,256]{3,2,1,0:T(8,128)(2,1)}), bf16[32,2,128,256]{3,2,1,0:T(8,128)(2,1)}, u32[]{:S(2)}, u32[]{:S(2)}) async-start(bf16[32,2,128,256]{3,2,1,0:T(8,128)(2,1)} %copy.72), calls=%async_computation.2 | async-start | bytes 8388608 | tf_op jit(solution)/shard_map/all_to_all | solution.py:145
  156.2 1.6 fusion.7
  157.8 2.4 %copy.74 = bf16[24,2,128,256]{3,2,1,0:T(8,128)(2,1)} copy(bf16[24,2,128,256]{3,0,2,1:T(8,128)(2,1)S(1)} %fusion.7) | data formatting | bytes 6291456
  161.6 49.1 %all-to-all-done.1 = bf16[32,2,128,256]{3,2,1,0:T(8,128)(2,1)} async-done(((bf16[32,2,128,256]{3,2,1,0:T(8,128)(2,1)}), bf16[32,2,128,256]{3,2,1,0:T(8,128)(2,1)}, u32[]{:S(2)}, u32[]{:S(2)}) %all-to-all-start.1) | async-done | bytes 4194336 | tf_op jit(solution)/shard_map/all_to_all | solution.py:145
  211.9 1.8 add_convert_fusion.2
  213.7 4.8 %copy.120 = bf16[32,2,128,256]{3,2,1,0:T(8,128)(2,1)} copy(bf16[32,2,128,256]{3,2,1,0:T(8,128)(2,1)} %all-to-all-done.1) | data formatting | bytes 8388608
  (84 shorter events, 16.4 us)
Async XLA Ops:
  7.2 4.0 %copy-start = (bf16[3,2048,256]{2,1,0:T(8,128)(2,1)S(1)}, bf16[3,2048,256]{2,1,0:T(8,128)(2,1)}, u32[]{:S(2)}) copy-start(bf16[3,2048,256]{2,1,0:T(8,128)(2,1)} %param.20) | copy-start | bytes 9437188
  7.2 5.7 %copy-start.15 = (f32[3,256]{1,0:T(4,128)S(1)}, f32[3,256]{1,0:T(4,128)}, u32[]{:S(2)}) copy-start(f32[3,256]{1,0:T(4,128)} %param.21) | copy-start | bytes 9220
  7.2 47.9 %all-gather.2.cloned.1.call-start = ((), (), s32[]{:S(2)}) async-start(), calls=%async_computation.3 | async-start | bytes 2949120 | tf_op jit(solution)/shard_map/all_gather | solution.py:85
  7.9 120.9 %all-reduce.2.cloned.1.call-start = ((), (), s32[]{:S(2)}) async-start(), calls=%async_computation.5 | async-start | bytes 327680 | tf_op jit(solution)/shard_map/psum | solution.py:134
  31.1 4.6 %copy-start.4 = (bf16[256,2048]{1,0:T(8,128)(2,1)S(1)}, bf16[256,2048]{1,0:T(8,128)(2,1)}, u32[]{:S(2)}) copy-start(bf16[256,2048]{1,0:T(8,128)(2,1)} %param.22) | copy-start | bytes 3145732
  31.1 5.8 %copy-start.16 = (s32[16,1]{0,1:T(1,128)S(1)}, s32[16,1]{0,1:T(1,128)}, u32[]{:S(2)}) copy-start(s32[16,1]{0,1:T(1,128)} %param.16) | copy-start | bytes 196
  31.1 6.1 %copy-start.14 = (s32[1,640]{1,0:T(1,128)S(1)}, s32[1,640]{1,0:T(1,128)}, u32[]{:S(2)}) copy-start(s32[1,640]{1,0:T(1,128)} %param.13) | copy-start | bytes 7684
  36.6 175.2 %reduce-scatter.2.cloned.1.call-start = ((), (), s32[]{:S(2)}) async-start(), calls=%async_computation.4 | async-start | bytes 2949120 | tf_op jit(solution)/shard_map/reduce_scatter | solution.py:106
  46.8 11.7 %copy-start.12 = (f32[2048]{0:T(1024)S(1)}, f32[2048]{0:T(1024)}, u32[]{:S(2)}) copy-start(f32[2048]{0:T(1024)} %param.19) | copy-start | bytes 24580
  55.1 2.5 %copy-start.3 = (bf16[640,2048]{1,0:T(8,128)(2,1)S(1)}, bf16[640,2048]{1,0:T(8,128)(2,1)}, u32[]{:S(2)}) copy-start(bf16[640,2048]{1,0:T(8,128)(2,1)} %all-gather.2.cloned.1.call-done) | copy-start | bytes 7864324
  55.1 3.4 %copy-start.13 = (f32[2048]{0:T(1024)S(1)}, f32[2048]{0:T(1024)}, u32[]{:S(2)}) copy-start(f32[2048]{0:T(1024)} %param.18) | copy-start | bytes 24580
  62.2 1.0 copy-start.10
  65.2 1.2 copy-start.5
  66.4 62.4 %copy-start.6 = (bf16[40,2048]{1,0:T(8,128)(2,1)S(1)}, bf16[40,2048]{1,0:T(8,128)(2,1)}, u32[]{:S(2)}) copy-start(bf16[40,2048]{1,0:T(8,128)(2,1)} %param.14) | copy-start | bytes 491524
  66.4 62.4 %copy-start.11 = (f32[2048]{0:T(1024)S(1)}, f32[2048]{0:T(1024)}, u32[]{:S(2)}) copy-start(f32[2048]{0:T(1024)} %param.23) | copy-start | bytes 24580
  68.8 72.9 %copy-start.2 = (bf16[40,1,128,256]{3,0,2,1:T(8,128)(2,1)S(1)}, bf16[40,1,128,256]{3,0,2,1:T(8,128)(2,1)}, u32[]{:S(2)}) copy-start(bf16[40,1,128,256]{3,0,2,1:T(8,128)(2,1)} %get-tuple-element.50) | copy-start | bytes 7864324
  129.8 0.7 copy-start.8
  134.3 14.5 %all-to-all-start = ((bf16[32,2,1024]{2,1,0:T(2,128)(2,1)}), bf16[32,2,1024]{2,1,0:T(2,128)(2,1)S(1)}, u32[]{:S(2)}, u32[]{:S(2)}) async-start(bf16[32,2,1024]{2,1,0:T(2,128)(2,1)} %reshape.267), calls=%async_computation.1 | async-start | bytes 262144 | tf_op jit(solution)/shard_map/all_to_all | solution.py:146
  148.7 62.0 %all-to-all-start.1 = ((bf16[32,2,128,256]{3,2,1,0:T(8,128)(2,1)}), bf16[32,2,128,256]{3,2,1,0:T(8,128)(2,1)}, u32[]{:S(2)}, u32[]{:S(2)}) async-start(bf16[32,2,128,256]{3,2,1,0:T(8,128)(2,1)} %copy.72), calls=%async_computation.2 | async-start | bytes 8388608 | tf_op jit(solution)/shard_map/all_to_all | solution.py:145
  157.8 2.4 %copy-start.9 = (bf16[40,2048]{1,0:T(8,128)(2,1)S(1)}, bf16[40,2048]{1,0:T(8,128)(2,1)}, u32[]{:S(2)}) copy-start(bf16[40,2048]{1,0:T(8,128)(2,1)} %copy-done.8) | copy-start | bytes 491524
  160.1 51.7 %copy-start.7 = (bf16[80,2048]{1,0:T(8,128)(2,1)S(1)}, bf16[80,2048]{1,0:T(8,128)(2,1)}, u32[]{:S(2)}) copy-start(bf16[80,2048]{1,0:T(8,128)(2,1)} %param.12) | copy-start | bytes 983044
  213.7 4.9 %copy-start.1 = (bf16[3,2048,256]{2,1,0:T(8,128)(2,1)S(1)}, bf16[3,2048,256]{2,1,0:T(8,128)(2,1)}, u32[]{:S(2)}) copy-start(bf16[3,2048,256]{2,1,0:T(8,128)(2,1)} %param.20) | copy-start | bytes 9437188
Sparse Core Ops, SparseCore 0:
  9.8 45.1 all-gather.1
  58.0 70.8 all-reduce.1
  131.6 42.1 reduce-scatter.1
where the time goes:
time: 226 us; the launch traced here: 225 us
  waiting for transfers between devices  118 us (52%)
  local copies, waits for them, and re-layouts  34.1 us (15%)
  other arithmetic  24.3 us (11%)
  matrix products  19.4 us (9%)
  starting transfers between devices  15.1 us (7%)
  between operations  14.1 us (6%)
    psum x1, waiting for transfers between devices, on_device(): lax.psum(partial_value.astype(jnp.bfloat16), 'tp').astype(jnp.float32)  60 us
    all_to_all x1, waiting for transfers between devices, on_device(): lax.all_to_all(send_cache, 'rep', split_axis=0, concat_axis=0, tiled=True)  49.1 us
    unnamed x40, local copies, waits for them, and re-layouts  12.8 us
    select_n x1, other arithmetic, decode_partial(): new_values = jnp.where(written, value_new[:, None, :], cache[:, 1])  8.49 us
    all_gather x1, waiting for transfers between devices, on_device(): lax.all_gather(prompt_rows, 'tp', axis=0, tiled=True)  8.31 us
    all_to_all x1, starting transfers between devices, on_device(): lax.all_to_all(send_cache, 'rep', split_axis=0, concat_axis=0, tiled=True)  7.44 us
    all_to_all x1, starting transfers between devices, on_device(): lax.all_to_all(send_rows, 'rep', split_axis=0, concat_axis=0, tiled=True)  7.41 us
    slice x1, local copies, waits for them, and re-layouts, decode_partial(): old_keys = cache[:, 0].reshape(count, length, heads_here, HEAD_DIM)  5.54 us
  transfers between devices with their start and end apart: 5, of which 3 were waited for; matrix products, arithmetic and copies ran while one was open for 31% of the time, Pallas kernels for 0%

commit v1 on v0

--- a/solution.py
+++ b/solution.py
@@ -6,6 +6,7 @@
 HEAD_DIM = 128
 CAP = 1
 EPSILON = 1e-05
+attach_the_slot = lambda mine, bus_axis: jax.lax.all_gather(mine, axis_name=bus_axis).sum(axis=0)
 
 
 def layer_norm(values, norm_gain, norm_bias):
@@ -131,7 +132,7 @@
         qkv_bias,
         out_weight,
     )
-    summed = lax.psum(partial_value.astype(jnp.bfloat16), "tp").astype(jnp.float32)
+    summed = attach_the_slot(partial_value.astype(jnp.bfloat16), "tp").astype(jnp.float32)
     decode_out = (decode_rows.astype(jnp.float32) + summed + out_bias).astype(jnp.bfloat16)
     kept_out = decode_out[:staying]
     kept_cache = updated[:staying]

time: 226 us -> 195 us (0.86)
  waiting for transfers between devices: 118 us -> 84.6 us
    psum x1 -> x0, waiting for transfers between devices: 60 us -> none  [on_device(): lax.psum(partial_value.astype(jnp.bfloat16), 'tp').astype(jnp.float32)]
    all_gather x0 -> x1, waiting for transfers between devices: none -> 26.5 us  [jax.lax.all_gather(mine, axis_name=bus_axis).sum(axis=0)]
  transfers between devices with their start and end apart: 5 -> 5, of which waited for: 3 -> 3; matrix products, arithmetic and copies ran while one was open for 31% -> 37% of each run, Pallas kernels for 0% -> 0%
where the time goes in v1:
time: 195 us; the launch traced here: 194 us
  waiting for transfers between devices  84.6 us (43%)
  local copies, waits for them, and re-layouts  34.1 us (17%)
  other arithmetic  26.5 us (14%)
  matrix products  19.4 us (10%)
  starting transfers between devices  15.1 us (8%)
  between operations  14.1 us (7%)
    all_to_all x1, waiting for transfers between devices, on_device(): lax.all_to_all(send_cache, 'rep', split_axis=0, concat_axis=0, tiled=True)  49.1 us
    all_gather x1, waiting for transfers between devices, jax.lax.all_gather(mine, axis_name=bus_axis).sum(axis=0)  26.5 us
    unnamed x40, local copies, waits for them, and re-layouts  12.8 us
    select_n x1, other arithmetic, decode_partial(): new_values = jnp.where(written, value_new[:, None, :], cache[:, 1])  8.49 us
    all_gather x1, waiting for transfers between devices, on_device(): lax.all_gather(prompt_rows, 'tp', axis=0, tiled=True)  8.31 us
    all_to_all x1, starting transfers between devices, on_device(): lax.all_to_all(send_cache, 'rep', split_axis=0, concat_axis=0, tiled=True)  7.44 us
    all_to_all x1, starting transfers between devices, on_device(): lax.all_to_all(send_rows, 'rep', split_axis=0, concat_axis=0, tiled=True)  7.4 us
    slice x1, local copies, waits for them, and re-layouts, decode_partial(): old_keys = cache[:, 0].reshape(count, length, heads_here, HEAD_DIM)  5.54 us
  transfers between devices with their start and end apart: 5, of which 3 were waited for; matrix products, arithmetic and copies ran while one was open for 37% of the time, Pallas kernels for 0%

profile of v1, /device:TPU:8, one launch (start us, length us, event | category | flops | bytes accessed | tf_op | source)
XLA Modules:
  0.0 193.8 jit_solution(13599956056124444567)
XLA Ops:
  11.1 1.6 convolution_bitcast_fusion
  13.1 5.5 %fusion.71 = (bf16[40,1,128,256]{3,2,1,0:T(8,128)(2,1)}, bf16[40,1,128,256]{3,2,1,0:T(8,128)(2,1)}) fusion(bf16[40,2,128,256]{3,2,1,0:T(8,128)(2,1)} %param.17), kind=kLoop, calls=%fused_computation.117 | loop fusion | bytes 10485760 | tf_op jit(solution)/shard_map/slice | solution.py:32
  18.6 4.4 %copy.84 = bf16[40,1,128,256]{2,3,0,1:T(8,128)(2,1)} copy(bf16[40,1,128,256]{3,2,1,0:T(8,128)(2,1)} %get-tuple-element.36) | data formatting | bytes 5242880 | tf_op jit(solution)/shard_map/reshape;squeeze | solution.py:32
  23.0 2.6 %fusion.53 = f32[40,2,1,128]{3,2,1,0:T(1,128)S(1)} fusion(bf16[40,128,2,128]{1,3,2,0:T(8,128)(2,1)} %bitcast.76, bf16[40,2,128,1]{2,1,0,3:T(2,128)(2,1)S(1)} %get-tuple-element.49), kind=kOutput, calls=%fused_computation.82 | convolution fusion | flops 2621440 | bytes 2682880 | tf_op jit(solution)/shard_map/rhe,rlhe->rhl/dot_general | solution.py:36
  26.1 4.9 %reshape.267 = bf16[40,128,2,128]{3,2,1,0:T(2,128)(2,1)} reshape(bf16[40,1,128,256]{3,2,1,0:T(8,128)(2,1)} %get-tuple-element.37) | data formatting | bytes 5242880 | tf_op jit(solution)/shard_map/reshape;squeeze | solution.py:33
  31.1 4.4 %fusion.11 = f32[40,2,1,128]{3,2,1,0:T(1,128)S(1)} fusion(bf16[40,2,128,1]{2,0,1,3:T(8,128)(2,1)S(1)} %fusion.59, bf16[40,128,2,128]{3,2,1,0:T(2,128)(2,1)} %reshape.267), kind=kOutput, calls=%fused_computation.20 | convolution fusion | flops 2621440 | bytes 2682880 | tf_op jit(solution)/shard_map/rhl,rlhe->rhe/dot_general | solution.py:53
  38.3 8.5 %broadcast_select_fusion = (bf16[40,1,128,256]{3,0,2,1:T(8,128)(2,1)}, bf16[40,1,128,256]{3,0,2,1:T(8,128)(2,1)}) fusion(pred[40,128]{0,1:T(8,128)(4,1)S(1)} %get-tuple-element.57, bf16[40,256]{1,0:T(8,128)(2,1)S(1)} %get-tuple-element.43, bf16[40,1,128,256]{3,2,1,0:T(8,128)(2,1)} %get-tuple-element.37, bf16[40,1,128,256]{3,2,1,0:T(8,128)(2,1)} %get-tuple-element.36, ...), kind=kLoop, calls=%fused_computation.26 | loop fusion | flops 2621440 | bytes 10531840 | tf_op jit(solution)/shard_map/jit(_where)/select_n | solution.py:61
  46.8 8.3 %all-gather.4.cloned.1.call-done = bf16[640,2048]{1,0:T(8,128)(2,1)} async-done(((bf16[80,2048]{1,0:T(8,128)(2,1)}), bf16[640,2048]{1,0:T(8,128)(2,1)}) %all-gather.4.cloned.1.call-update) | async-done | bytes 2621456 | tf_op jit(solution)/shard_map/all_gather | solution.py:86
  55.1 2.3 %convert_reduce_fusion = f32[640]{0:T(1024)S(1)} fusion(bf16[640,2048]{1,0:T(8,128)(2,1)} %all-gather.4.cloned.1.call-done), kind=kLoop, calls=%fused_computation.2 | loop fusion | flops 2620800 | bytes 2624000 | tf_op jit(solution)/shard_map/reduce_sum | solution.py:14
  58.4 3.1 %fusion.25 = f32[3,640,256]{1,2,0:T(8,128)S(1)} fusion(bf16[3,2048,256]{2,1,0:T(8,128)(2,1)S(1)} %copy-done, bf16[640,2048]{1,0:T(8,128)(2,1)S(1)} %copy-done.3, f32[2048]{0:T(1024)S(1)} %copy-done.12, f32[2048]{0:T(1024)S(1)} %copy-done.13, f32[640]{0:T(1024)S(1)} %add_rsqrt_fusion, f32[640]{0:T(1024)S(1)} %broadcast_multiply_fusion), kind=kOutput, calls=%fused_computation.39 | convolution fusion | flops 2021130240 | bytes 7754752 | tf_op jit(solution)/shard_map/rd,cde->cre/dot_general | solution.py:87
  63.2 2.0 %fusion.74 = (f32[2,640]{1,0:T(2,128)S(1)}, f32[2,640,640]{1,2,0:T(8,128)S(1)}) fusion(f32[2,640,640]{1,2,0:T(8,128)S(1)} %fusion.38, pred[640,640]{0,1:T(8,128)(4,1)S(1)} %copy-done.10), kind=kOutput, calls=%fused_computation.120 | output fusion | flops 4915839 | bytes 6968320 | tf_op jit(solution)/shard_map/sub | solution.py:103
  66.4 2.4 %convolution_convert_fusion = bf16[640,2048]{1,0:T(8,128)(2,1)} fusion(bf16[640,256]{0,1:T(8,128)(2,1)S(1)} %bitcast.80, bf16[256,2048]{1,0:T(8,128)(2,1)S(1)} %copy-done.5), kind=kOutput, calls=%fused_computation.14 | convolution fusion | flops 672399360 | bytes 3997696 | tf_op jit(solution)/shard_map/dot_general | solution.py:108
  68.9 26.5 %all-gather.6.cloned.1.call-done = bf16[320,2048]{1,0:T(8,128)(2,1)} async-done(((bf16[40,2048]{1,0:T(8,128)(2,1)}), bf16[320,2048]{1,0:T(8,128)(2,1)}) %all-gather.6.cloned.1.call-update) | async-done | bytes 1310736 | tf_op jit(solution)/shard_map/all_gather | solution.py:9
  95.4 2.2 %reduce_sum.91 = bf16[40,2048]{1,0:T(8,128)(2,1)} reduce(bf16[8,40,2048]{2,1,0:T(8,128)(2,1)} %bitcast.79, bf16[]{:T(256)} %constant.22.clone.1), dimensions={0}, to_apply=%region_10.11 | reduce | flops 573440 | bytes 1474562 | tf_op jit(solution)/shard_map/reduce_sum | solution.py:9
  101.4 1.6 reshape.268
  103.0 7.4 %all-to-all-start = ((bf16[32,2,1024]{2,1,0:T(2,128)(2,1)}), bf16[32,2,1024]{2,1,0:T(2,128)(2,1)S(1)}, u32[]{:S(2)}, u32[]{:S(2)}) async-start(bf16[32,2,1024]{2,1,0:T(2,128)(2,1)} %reshape.268), calls=%async_computation.1 | async-start | bytes 262144 | tf_op jit(solution)/shard_map/all_to_all | solution.py:147
  110.5 2.6 %convolution_convert_fusion.1 = bf16[32,2,128,256]{3,0,2,1:T(8,128)(2,1)S(1)} fusion(bf16[40,1,128,256]{3,0,2,1:T(8,128)(2,1)S(1)} %copy-done.2, bf16[40,1,128,256]{3,0,2,1:T(8,128)(2,1)} %get-tuple-element.51, s32[16]{0:T(128)S(1)} %convert_add_fusion.1), kind=kOutput, calls=%fused_computation.16 | convolution fusion | flops 73400832 | bytes 9437248 | tf_op jit(solution)/shard_map/so,oklh->sklh/dot_general | solution.py:139
  113.1 4.4 %copy.72 = bf16[32,2,128,256]{3,2,1,0:T(8,128)(2,1)} copy(bf16[32,2,128,256]{3,0,2,1:T(8,128)(2,1)S(1)} %convolution_convert_fusion.1) | data formatting | bytes 8388608 | tf_op jit(solution)/shard_map/convert_element_type | solution.py:141
  117.5 7.4 %all-to-all-start.1 = ((bf16[32,2,128,256]{3,2,1,0:T(8,128)(2,1)}), bf16[32,2,128,256]{3,2,1,0:T(8,128)(2,1)}, u32[]{:S(2)}, u32[]{:S(2)}) async-start(bf16[32,2,128,256]{3,2,1,0:T(8,128)(2,1)} %copy.72), calls=%async_computation.2 | async-start | bytes 8388608 | tf_op jit(solution)/shard_map/all_to_all | solution.py:146
  124.9 1.6 fusion.7
  126.5 2.4 %copy.74 = bf16[24,2,128,256]{3,2,1,0:T(8,128)(2,1)} copy(bf16[24,2,128,256]{3,0,2,1:T(8,128)(2,1)S(1)} %fusion.7) | data formatting | bytes 6291456
  130.4 49.1 %all-to-all-done.1 = bf16[32,2,128,256]{3,2,1,0:T(8,128)(2,1)} async-done(((bf16[32,2,128,256]{3,2,1,0:T(8,128)(2,1)}), bf16[32,2,128,256]{3,2,1,0:T(8,128)(2,1)}, u32[]{:S(2)}, u32[]{:S(2)}) %all-to-all-start.1) | async-done | bytes 4194336 | tf_op jit(solution)/shard_map/all_to_all | solution.py:146
  180.6 1.8 add_convert_fusion.2
  182.4 4.8 %copy.119 = bf16[32,2,128,256]{3,2,1,0:T(8,128)(2,1)} copy(bf16[32,2,128,256]{3,2,1,0:T(8,128)(2,1)} %all-to-all-done.1) | data formatting | bytes 8388608
  (85 shorter events, 17.7 us)
Async XLA Ops:
  7.2 4.0 %copy-start = (bf16[3,2048,256]{2,1,0:T(8,128)(2,1)S(1)}, bf16[3,2048,256]{2,1,0:T(8,128)(2,1)}, u32[]{:S(2)}) copy-start(bf16[3,2048,256]{2,1,0:T(8,128)(2,1)} %param.20) | copy-start | bytes 9437188
  7.2 5.7 %copy-start.15 = (f32[3,256]{1,0:T(4,128)S(1)}, f32[3,256]{1,0:T(4,128)}, u32[]{:S(2)}) copy-start(f32[3,256]{1,0:T(4,128)} %param.21) | copy-start | bytes 9220
  7.2 47.9 %all-gather.4.cloned.1.call-start = ((), (), s32[]{:S(2)}) async-start(), calls=%async_computation.3 | async-start | bytes 2949120 | tf_op jit(solution)/shard_map/all_gather | solution.py:86
  7.9 87.5 %all-gather.6.cloned.1.call-start = ((), (), s32[]{:S(2)}) async-start(), calls=%async_computation.5 | async-start | bytes 1474560 | tf_op jit(solution)/shard_map/all_gather | solution.py:9
  31.1 4.6 %copy-start.4 = (bf16[256,2048]{1,0:T(8,128)(2,1)S(1)}, bf16[256,2048]{1,0:T(8,128)(2,1)}, u32[]{:S(2)}) copy-start(bf16[256,2048]{1,0:T(8,128)(2,1)} %param.22) | copy-start | bytes 3145732
  31.1 5.8 %copy-start.16 = (s32[16,1]{0,1:T(1,128)S(1)}, s32[16,1]{0,1:T(1,128)}, u32[]{:S(2)}) copy-start(s32[16,1]{0,1:T(1,128)} %param.16) | copy-start | bytes 196
  31.1 6.1 %copy-start.14 = (s32[1,640]{1,0:T(1,128)S(1)}, s32[1,640]{1,0:T(1,128)}, u32[]{:S(2)}) copy-start(s32[1,640]{1,0:T(1,128)} %param.13) | copy-start | bytes 7684
  36.6 144.0 %reduce-scatter.2.cloned.1.call-start = ((), (), s32[]{:S(2)}) async-start(), calls=%async_computation.4 | async-start | bytes 2949120 | tf_op jit(solution)/shard_map/reduce_scatter | solution.py:107
  46.8 11.7 %copy-start.12 = (f32[2048]{0:T(1024)S(1)}, f32[2048]{0:T(1024)}, u32[]{:S(2)}) copy-start(f32[2048]{0:T(1024)} %param.19) | copy-start | bytes 24580
  55.1 2.5 %copy-start.3 = (bf16[640,2048]{1,0:T(8,128)(2,1)S(1)}, bf16[640,2048]{1,0:T(8,128)(2,1)}, u32[]{:S(2)}) copy-start(bf16[640,2048]{1,0:T(8,128)(2,1)} %all-gather.4.cloned.1.call-done) | copy-start | bytes 7864324
  55.1 3.4 %copy-start.13 = (f32[2048]{0:T(1024)S(1)}, f32[2048]{0:T(1024)}, u32[]{:S(2)}) copy-start(f32[2048]{0:T(1024)} %param.18) | copy-start | bytes 24580
  62.2 1.0 copy-start.10
  65.2 1.2 copy-start.5
  68.8 28.8 %copy-start.6 = (bf16[40,2048]{1,0:T(8,128)(2,1)S(1)}, bf16[40,2048]{1,0:T(8,128)(2,1)}, u32[]{:S(2)}) copy-start(bf16[40,2048]{1,0:T(8,128)(2,1)} %param.14) | copy-start | bytes 491524
  68.8 28.8 %copy-start.11 = (f32[2048]{0:T(1024)S(1)}, f32[2048]{0:T(1024)}, u32[]{:S(2)}) copy-start(f32[2048]{0:T(1024)} %param.23) | copy-start | bytes 24580
  68.8 41.6 %copy-start.2 = (bf16[40,1,128,256]{3,0,2,1:T(8,128)(2,1)S(1)}, bf16[40,1,128,256]{3,0,2,1:T(8,128)(2,1)}, u32[]{:S(2)}) copy-start(bf16[40,1,128,256]{3,0,2,1:T(8,128)(2,1)} %get-tuple-element.50) | copy-start | bytes 7864324
  98.6 0.7 copy-start.8
  103.0 14.5 %all-to-all-start = ((bf16[32,2,1024]{2,1,0:T(2,128)(2,1)}), bf16[32,2,1024]{2,1,0:T(2,128)(2,1)S(1)}, u32[]{:S(2)}, u32[]{:S(2)}) async-start(bf16[32,2,1024]{2,1,0:T(2,128)(2,1)} %reshape.268), calls=%async_computation.1 | async-start | bytes 262144 | tf_op jit(solution)/shard_map/all_to_all | solution.py:147
  117.5 62.0 %all-to-all-start.1 = ((bf16[32,2,128,256]{3,2,1,0:T(8,128)(2,1)}), bf16[32,2,128,256]{3,2,1,0:T(8,128)(2,1)}, u32[]{:S(2)}, u32[]{:S(2)}) async-start(bf16[32,2,128,256]{3,2,1,0:T(8,128)(2,1)} %copy.72), calls=%async_computation.2 | async-start | bytes 8388608 | tf_op jit(solution)/shard_map/all_to_all | solution.py:146
  126.5 2.4 %copy-start.9 = (bf16[40,2048]{1,0:T(8,128)(2,1)S(1)}, bf16[40,2048]{1,0:T(8,128)(2,1)}, u32[]{:S(2)}) copy-start(bf16[40,2048]{1,0:T(8,128)(2,1)} %copy-done.8) | copy-start | bytes 491524
  128.9 51.7 %copy-start.7 = (bf16[80,2048]{1,0:T(8,128)(2,1)S(1)}, bf16[80,2048]{1,0:T(8,128)(2,1)}, u32[]{:S(2)}) copy-start(bf16[80,2048]{1,0:T(8,128)(2,1)} %param.12) | copy-start | bytes 983044
  182.4 4.9 %copy-start.1 = (bf16[3,2048,256]{2,1,0:T(8,128)(2,1)S(1)}, bf16[3,2048,256]{2,1,0:T(8,128)(2,1)}, u32[]{:S(2)}) copy-start(bf16[3,2048,256]{2,1,0:T(8,128)(2,1)} %param.20) | copy-start | bytes 9437188
Sparse Core Ops, SparseCore 0:
  9.8 45.1 all-gather.3
  57.4 37.9 all-gather.5
  98.0 42.7 reduce-scatter.1
